TPU v7x, 256 devices: a whole 4x4x8 slice. The times are simulated.
256 devices in a mesh: section: 2 (over core), patch: 4 (over y), req: 32 (over z, x).
Axes of the slice: x: 4, y: 4, z: 8, core: 2. Of those that a mesh axis runs over, the one named last changes fastest.
Arguments:
- hidden: bfloat16 [64, 1024, 1536], P('req', 'patch'), may hold values from -6 to 6
- w_qkv: bfloat16 [2, 1536, 2304], P('section', ('patch', 'req')), may hold values from -0.15625 to 0.15625
- w_out: bfloat16 [2, 768, 1536], P('section', ('patch', 'req')), may hold values from -0.21875 to 0.21875
- modulation: float32 [2, 64, 3, 1536], P('section', 'req'), may hold values from -3 to 3
- text_kv: bfloat16 [2, 64, 160, 1536], P('section', 'req'), may hold values from -1000 to 1000
- text_lengths: int32 [64], P('req'), may hold values from 77 to 154, as said below
- stale_kv: bfloat16 [2, 64, 1024, 1536], P('section', 'req', 'patch'), may hold values from -48 to 48
- held_hidden: bfloat16 [2, 64, 96, 1536], P('section', 'req', 'patch'), may hold values from -6 to 6
- recompute_rows: int32 [2, 64, 96], P('section', 'req', 'patch'), may hold values from 0 to 255, as said below
- coefficients: float32 [64, 2], P('req'), may hold values from 0.5 to 1.5
Outputs:
- latents: float32 [64, 1024, 1536], P('req', 'patch', 'section')
- cache: bfloat16 [2, 64, 1024, 1536], P('section', 'req', 'patch')
Inputs may be any that keep to these rules, and one draw needn't show every extreme that they name: `text_lengths`: some request has exactly 154 text tokens and some exactly 77. `recompute_rows`: the row numbers listed for one layer, request and patch are distinct.
All inputs are finite; a program needn't handle non-finite values.
Results may differ from a plain program's by a relative error of at most 0.025.
Values may be sent and summed in bfloat16 or wider, within the bound.
No kernel may reach another device: no remote copies, remote signals or barrier semaphores. Data moves between devices by JAX's collectives and lax.ppermute only.
A program may use at most 128 MiB of HBM per device.

v0:
```python
import jax
import jax.numpy as jnp
from jax import lax
from jax.sharding import PartitionSpec as P

HEADS = 12
norm_eps = 1e-06
score_scale = 0.125


def shifted(block, axis, distance):
    devices = range(lax.axis_size(axis))
    route = [(i - distance, i) for i in devices if i - distance in devices]
    return lax.ppermute(block, axis, route)


def modulate(row_block, shift_row, scale_row):
    values = row_block.astype(jnp.float32)
    centre = values - jnp.mean(values, axis=-1, keepdims=True)
    spread = jnp.mean(centre * centre, axis=-1, keepdims=True)
    return (centre * lax.rsqrt(spread + norm_eps) * (1.0 + scale_row) + shift_row).astype(
        jnp.bfloat16
    )


def attend(queries, key_rows, value_rows, usable):
    row_count = queries.shape[0]
    feature_count = queries.shape[1]
    query_heads = queries.reshape(row_count, HEADS, feature_count // HEADS)
    key_heads = key_rows.reshape(key_rows.shape[0], HEADS, feature_count // HEADS)
    value_heads = value_rows.reshape(value_rows.shape[0], HEADS, feature_count // HEADS)
    scores = (
        jnp.einsum("qhd,khd->hqk", query_heads, key_heads, preferred_element_type=jnp.float32)
        * score_scale
    )
    scores = jnp.where(usable[None, None, :], scores, -1e30)
    row_max = jnp.max(scores, axis=-1, keepdims=True)
    exp_scores = jnp.exp(scores - row_max)
    soft_weights = (exp_scores / jnp.sum(exp_scores, axis=-1, keepdims=True)).astype(jnp.bfloat16)
    attended = jnp.einsum(
        "hqk,khd->qhd", soft_weights, value_heads, preferred_element_type=jnp.float32
    )
    return attended.reshape(row_count, feature_count).astype(jnp.bfloat16)


def body(
    hidden,
    w_qkv,
    w_out,
    modulation,
    text_kv,
    text_lengths,
    stale_kv,
    held_hidden,
    recompute_rows,
    coefficients,
):
    full_qkv, full_out = (
        lax.all_gather(w_qkv[0], ("patch", "req"), axis=0, tiled=True),
        lax.all_gather(w_out[0], ("patch", "req"), axis=0, tiled=True),
    )
    section_index = lax.axis_index("section")
    patch_index = lax.axis_index("patch")
    request_count = hidden.shape[0]
    patch_rows = hidden.shape[1]
    model_width = hidden.shape[2]
    head_width = full_out.shape[0]
    text_slots = text_kv.shape[2]

    def process(layer_input, slot_index):
        mod_rows = lax.dynamic_index_in_dim(modulation[0], slot_index, 0, keepdims=False)
        text_rows = lax.dynamic_index_in_dim(text_kv[0], slot_index, 0, keepdims=False)
        text_count = lax.dynamic_index_in_dim(text_lengths, slot_index, 0, keepdims=False)
        stale_block = lax.dynamic_index_in_dim(stale_kv[0], slot_index, 0, keepdims=False)
        held_rows = lax.dynamic_index_in_dim(held_hidden[0], slot_index, 0, keepdims=False)
        redo_index = lax.dynamic_index_in_dim(recompute_rows[0], slot_index, 0, keepdims=False)
        held_norm = modulate(held_rows, mod_rows[0], mod_rows[1])
        redone = jnp.dot(
            held_norm, full_qkv[:, head_width:], preferred_element_type=jnp.float32
        ).astype(jnp.bfloat16)
        patched = stale_block.at[redo_index].set(redone)
        image_rows = lax.all_gather(patched, "patch", axis=0, tiled=True)
        normed = modulate(layer_input, mod_rows[0], mod_rows[1])
        projected = jnp.dot(normed, full_qkv, preferred_element_type=jnp.float32).astype(
            jnp.bfloat16
        )
        fresh_rows = projected[:, head_width:]
        image_rows = lax.dynamic_update_slice_in_dim(
            image_rows, fresh_rows, patch_index * patch_rows, 0
        )
        context = jnp.concatenate([text_rows, image_rows], axis=0)
        usable = jnp.concatenate(
            [jnp.arange(text_slots) < text_count, jnp.ones((image_rows.shape[0],), jnp.bool_)]
        )
        attended = attend(
            projected[:, :head_width], context[:, :head_width], context[:, head_width:], usable
        )
        update = jnp.dot(attended, full_out, preferred_element_type=jnp.float32)
        layer_out = (layer_input.astype(jnp.float32) + mod_rows[2] * update).astype(jnp.bfloat16)
        return (layer_out, fresh_rows)

    first_pass = [process(hidden[slot_number], slot_number) for slot_number in range(request_count)]
    first_out = jnp.stack([entry[0] for entry in first_pass])
    first_fresh = jnp.stack([entry[1] for entry in first_pass])
    received = shifted(first_out, "section", 1)
    second_pass = [
        process(received[slot_number], slot_number) for slot_number in range(request_count)
    ]
    second_out = jnp.stack([entry[0] for entry in second_pass])
    second_fresh = jnp.stack([entry[1] for entry in second_pass])
    fresh_all = jnp.where(section_index == 0, first_fresh, second_fresh)
    half_width = model_width // 2
    returned = shifted(second_out[:, :, :half_width], "section", -1)
    own_half = jnp.where(section_index == 0, returned, second_out[:, :, half_width:])
    source_half = lax.dynamic_slice_in_dim(hidden, section_index * half_width, half_width, 2)
    latents = coefficients[:, 0][:, None, None] * source_half.astype(jnp.float32) + coefficients[
        :, 1
    ][:, None, None] * own_half.astype(jnp.float32)
    return (latents, fresh_all[None])


def solution(mesh):
    return jax.shard_map(
        body,
        mesh=mesh,
        in_specs=(
            P("req", "patch", None),
            P("section", ("patch", "req"), None),
            P("section", ("patch", "req"), None),
            P("section", "req", None, None),
            P("section", "req", None, None),
            P("req"),
            P("section", "req", "patch", None),
            P("section", "req", "patch", None),
            P("section", "req", "patch"),
            P("req", None),
        ),
        out_specs=(P("req", "patch", "section"), P("section", "req", "patch", None)),
        check_vma=False,
    )
```

profile of v0, /device:TPU:1, one launch (start us, length us, event | category | flops | bytes accessed | tf_op | source)
XLA Modules:
  0.0 496.8 jit_solution(3415797970322674418)
XLA Ops:
  7.2 1.6 copy.50
  8.9 1.4 copy.54
  14.2 1.5 slice_bitcast_fusion
  15.7 140.7 %all-gather.11.cloned.1.call-done = bf16[1,1536,2304]{2,0,1:T(2,128)(2,1)} async-done(((bf16[1,12,2304]{2,0,1:T(2,128)(2,1)}), bf16[1,1536,2304]{2,0,1:T(2,128)(2,1)}) %all-gather.11.cloned.1.call-update) | async-done | bytes 7077904 | tf_op jit(solution)/shard_map/all_gather | solution.py:59
  156.4 9.0 %copy.67 = bf16[1,1536,2304]{2,1,0:T(8,128)(2,1)} copy(bf16[1,1536,2304]{2,0,1:T(2,128)(2,1)} %all-gather.11.cloned.1.call-done) | data formatting | bytes 14155776
  165.4 3.1 fusion.52
  170.7 3.2 fusion.55
  173.9 1.7 scatter_fusion.1
  179.3 1.2 slice_bitcast_fusion.7
  180.5 91.4 %all-gather.13.cloned.1.call-done = bf16[1,768,1536]{2,0,1:T(2,128)(2,1)} async-done(((bf16[1,6,1536]{2,0,1:T(2,128)(2,1)}), bf16[1,768,1536]{2,0,1:T(2,128)(2,1)}) %all-gather.13.cloned.1.call-update) | async-done | bytes 2359312 | tf_op jit(solution)/shard_map/all_gather | solution.py:60
  271.9 3.0 copy.65
  275.0 5.2 %convolution_convert_fusion.3 = bf16[256,2304]{1,0:T(8,128)(2,1)S(1)} fusion(bf16[1536,2304]{1,0:T(8,128)(2,1)} %bitcast.210, f32[1536]{0:T(1024)S(1)} %get-tuple-element.16, f32[1536]{0:T(1024)S(1)} %get-tuple-element.17, f32[256]{0:T(256)S(1)} %add_rsqrt_fusion.3, f32[256]{0:T(256)S(1)} %broadcast_multiply_fusion.3, bf16[2,256,1536]{2,1,0:T(8,128)(2,1)S(1)} %copy-done.1), kind=kOutput, calls=%fused_computation.46 | convolution fusion | flops 1814888448 | bytes 9062400 | tf_op jit(solution)/shard_map/dot_general | solution.py:84
  282.0 1.9 copy.52
  283.9 5.7 %convolution_convert_fusion.2 = bf16[256,2304]{1,0:T(8,128)(2,1)S(1)} fusion(bf16[1536,2304]{1,0:T(8,128)(2,1)} %bitcast.211, f32[1536]{0:T(1024)S(1)} %get-tuple-element.18, f32[1536]{0:T(1024)S(1)} %get-tuple-element.19, f32[256]{0:T(256)S(1)} %add_rsqrt_fusion.2, f32[256]{0:T(256)S(1)} %broadcast_multiply_fusion.2, bf16[2,256,1536]{2,1,0:T(8,128)(2,1)} %param.10), kind=kOutput, calls=%fused_computation.45 | convolution fusion | flops 1814888448 | bytes 9058304 | tf_op jit(solution)/shard_map/dot_general | solution.py:84
  291.4 1.9 copy.56
  293.3 23.1 %all-gather.7.cloned.1.call-done = bf16[1024,1536]{1,0:T(8,128)(2,1)} async-done(((bf16[256,1536]{1,0:T(8,128)(2,1)}), bf16[1024,1536]{1,0:T(8,128)(2,1)}) %all-gather.7.cloned.1.call-update) | async-done | bytes 3145744 | tf_op jit(solution)/shard_map/all_gather | solution.py:82
  316.4 3.9 copy.73
  321.3 2.1 pad_maximum_fusion.3
  323.4 3.9 copy.53
  327.3 4.0 copy.51
  331.3 29.1 %all-gather.9.cloned.1.call-done = bf16[1024,1536]{1,0:T(8,128)(2,1)} async-done(((bf16[256,1536]{1,0:T(8,128)(2,1)}), bf16[1024,1536]{1,0:T(8,128)(2,1)}) %all-gather.9.cloned.1.call-update) | async-done | bytes 3145744 | tf_op jit(solution)/shard_map/all_gather | solution.py:82
  360.4 3.9 copy.72
  365.4 2.0 pad_maximum_fusion.1
  367.4 3.9 copy.57
  371.4 4.1 copy.55
  375.4 6.9 %fusion.178 = f32[12,256]{1,0:T(8,128)S(1)} fusion(pred[1184]{0:T(1024)(128)(4,1)S(1)} %concatenate.35, bf16[256,12,64]{0,2,1:T(8,128)(2,1)} %bitcast.232, bf16[1184,12,64]{0,2,1:T(8,128)(2,1)} %bitcast.216), kind=kOutput, calls=%fused_computation.243 | convolution fusion | flops 480117920 | bytes 2225312 | tf_op jit(solution)/shard_map/sub | solution.py:38
  382.3 9.5 %fusion.93 = bf16[12,64,256]{2,1,0:T(8,128)(2,1)} fusion(bf16[1184,12,64]{0,2,1:T(8,128)(2,1)} %bitcast.218, f32[12,256]{1,0:T(8,128)S(1)} %fusion.178, pred[1184]{0:T(1024)(128)(4,1)S(1)} %concatenate.35, bf16[256,12,64]{0,2,1:T(8,128)(2,1)} %bitcast.233, bf16[1184,12,64]{0,2,1:T(8,128)(2,1)} %bitcast.217), kind=kOutput, calls=%fused_computation.131 | convolution fusion | flops 949522560 | bytes 4437152 | tf_op jit(solution)/shard_map/hqk,khd->qhd/dot_general | solution.py:40
  391.8 7.1 %fusion.177 = f32[12,256]{1,0:T(8,128)S(1)} fusion(pred[1184]{0:T(1024)(128)(4,1)S(1)} %concatenate.37, bf16[256,12,64]{0,2,1:T(8,128)(2,1)} %bitcast.234, bf16[1184,12,64]{0,2,1:T(8,128)(2,1)} %bitcast.223), kind=kOutput, calls=%fused_computation.242 | convolution fusion | flops 480117920 | bytes 2225312 | tf_op jit(solution)/shard_map/sub | solution.py:38
  398.9 9.4 %fusion.92 = bf16[12,64,256]{2,1,0:T(8,128)(2,1)} fusion(bf16[1184,12,64]{0,2,1:T(8,128)(2,1)} %bitcast.227, f32[12,256]{1,0:T(8,128)S(1)} %fusion.177, pred[1184]{0:T(1024)(128)(4,1)S(1)} %concatenate.37, bf16[256,12,64]{0,2,1:T(8,128)(2,1)} %bitcast.235, bf16[1184,12,64]{0,2,1:T(8,128)(2,1)} %bitcast.224), kind=kOutput, calls=%fused_computation.130 | convolution fusion | flops 949522560 | bytes 4437152 | tf_op jit(solution)/shard_map/hqk,khd->qhd/dot_general | solution.py:40
  408.3 2.2 fusion.39
  410.5 2.3 fusion.38
  413.0 1.3 collective-permute-start
  414.3 4.0 collective-permute-done
  419.2 2.2 convolution_convert_fusion
  422.7 2.2 convolution_convert_fusion.1
  426.0 3.5 pad_maximum_fusion
  429.5 4.0 copy.63
  433.7 4.1 copy.61
  437.7 4.0 copy.60
  441.9 4.1 copy.58
  446.0 6.7 %fusion.180 = f32[12,256]{1,0:T(8,128)S(1)} fusion(pred[1184]{0:T(1024)(128)(4,1)S(1)} %copy-done.30, bf16[256,12,64]{0,2,1:T(8,128)(2,1)S(1)} %bitcast.238, bf16[1184,12,64]{0,2,1:T(8,128)(2,1)} %bitcast.221), kind=kOutput, calls=%fused_computation.245 | convolution fusion | flops 480117920 | bytes 2225312 | tf_op jit(solution)/shard_map/sub | solution.py:38
  452.7 8.7 %fusion.90 = bf16[12,64,256]{2,1,0:T(8,128)(2,1)S(1)} fusion(bf16[1184,12,64]{0,2,1:T(8,128)(2,1)} %bitcast.225, f32[12,256]{1,0:T(8,128)S(1)} %fusion.180, pred[1184]{0:T(1024)(128)(4,1)S(1)} %copy-done.30, bf16[256,12,64]{0,2,1:T(8,128)(2,1)} %bitcast.239, bf16[1184,12,64]{0,2,1:T(8,128)(2,1)} %bitcast.222), kind=kOutput, calls=%fused_computation.128 | convolution fusion | flops 949522560 | bytes 4437152 | tf_op jit(solution)/shard_map/hqk,khd->qhd/dot_general | solution.py:40
  461.4 7.0 %fusion.179 = f32[12,256]{1,0:T(8,128)S(1)} fusion(pred[1184]{0:T(1024)(128)(4,1)S(1)} %copy-done.28, bf16[256,12,64]{0,2,1:T(8,128)(2,1)S(1)} %bitcast.236, bf16[1184,12,64]{0,2,1:T(8,128)(2,1)} %bitcast.219), kind=kOutput, calls=%fused_computation.244 | convolution fusion | flops 480117920 | bytes 2225312 | tf_op jit(solution)/shard_map/sub | solution.py:38
  468.4 9.3 %fusion.91 = bf16[12,64,256]{2,1,0:T(8,128)(2,1)} fusion(bf16[1184,12,64]{0,2,1:T(8,128)(2,1)} %bitcast.226, f32[12,256]{1,0:T(8,128)S(1)} %fusion.179, pred[1184]{0:T(1024)(128)(4,1)S(1)} %copy-done.28, bf16[256,12,64]{0,2,1:T(8,128)(2,1)S(1)} %bitcast.237, bf16[1184,12,64]{0,2,1:T(8,128)(2,1)} %bitcast.220), kind=kOutput, calls=%fused_computation.129 | convolution fusion | flops 949522560 | bytes 4437152 | tf_op jit(solution)/shard_map/hqk,khd->qhd/dot_general | solution.py:40
  477.7 2.1 fusion.36
  482.4 3.1 collective-permute-start.1
  485.8 2.7 maximum_select_fusion
  488.5 1.6 multiply_add_fusion
  (120 shorter events, 22.0 us)
Async XLA Ops:
  7.2 149.3 %all-gather.11.cloned.1.call-start = ((), (), s32[]{:S(2)}) async-start(), calls=%async_computation.2 | async-start | bytes 14266368 | tf_op jit(solution)/shard_map/all_gather | solution.py:59
  8.8 263.1 %all-gather.13.cloned.1.call-start = ((), (), s32[]{:S(2)}) async-start(), calls=%async_computation.3 | async-start | bytes 4755456 | tf_op jit(solution)/shard_map/all_gather | solution.py:60
  10.3 306.1 %all-gather.7.cloned.1.call-start = ((), (), s32[]{:S(2)}) async-start(), calls=%async_computation | async-start | bytes 3932160 | tf_op jit(solution)/shard_map/all_gather | solution.py:82
  15.7 149.7 %copy-start.23 = (bf16[1,2,24,1536]{3,2,1,0:T(8,128)(2,1)S(1)}, bf16[1,2,24,1536]{3,2,1,0:T(8,128)(2,1)}, u32[]{:S(2)}) copy-start(bf16[1,2,24,1536]{3,2,1,0:T(8,128)(2,1)} %param.17) | copy-start | bytes 442372
  169.7 0.9 copy-start.13
  170.6 189.7 %all-gather.9.cloned.1.call-start = ((), (), s32[]{:S(2)}) async-start(), calls=%async_computation.1 | async-start | bytes 3932160 | tf_op jit(solution)/shard_map/all_gather | solution.py:82
  173.9 2.6 copy-start.31
  173.9 4.5 copy-start
  175.6 0.9 copy-start.12
  177.8 204.5 %copy-start.27 = (pred[1184]{0:T(1024)(128)(4,1)}, pred[1184]{0:T(1024)(128)(4,1)S(1)}, u32[]{:S(2)}) copy-start(pred[1184]{0:T(1024)(128)(4,1)S(1)} %concatenate.35) | copy-start | bytes 3556
  178.4 220.5 %copy-start.29 = (pred[1184]{0:T(1024)(128)(4,1)}, pred[1184]{0:T(1024)(128)(4,1)S(1)}, u32[]{:S(2)}) copy-start(pred[1184]{0:T(1024)(128)(4,1)S(1)} %concatenate.37) | copy-start | bytes 3556
  271.9 3.0 copy-start.1
  280.2 1.0 copy-start.21
  289.6 1.0 copy-start.19
  316.4 3.9 copy-start.6
  316.4 3.9 copy-start.22
  360.4 3.9 copy-start.7
  360.4 3.9 copy-start.20
  408.3 2.2 copy-start.2
  408.3 10.9 %slice-start = ((s8[7077888]{0:T(1024)(128)(4,1)}), s8[4194304]{0:T(1024)(128)(4,1)S(1)}, s32[]{:S(2)}) async-start(s8[7077888]{0:T(1024)(128)(4,1)} %bitcast.212), calls=%async_computation.4 | async-start | bytes 8388608
  410.5 8.7 %slice-start.1 = ((s8[7077888]{0:T(1024)(128)(4,1)}), s8[2883584]{0:T(1024)(128)(4,1)S(1)}, s32[]{:S(2)}) async-start(s8[7077888]{0:T(1024)(128)(4,1)} %bitcast.212), calls=%async_computation.5 | async-start | bytes 5767168
  413.0 5.3 %collective-permute-start = (bf16[2,256,1536]{2,1,0:T(8,128)(2,1)S(1)}, bf16[2,256,1536]{2,1,0:T(8,128)(2,1)S(1)}, u32[]{:S(2)}, u32[]{:S(2)}) collective-permute-start(bf16[2,256,1536]{2,1,0:T(8,128)(2,1)S(1)} %pad_maximum_fusion.4), channel_id=1, source_target_pairs={{0,128},{1,129},{2,130},{3,131},{4,132},{5,133},{6,134},{7,135},{8... | collective-permute-start | bytes 4718600 | tf_op jit(solution)/shard_map/ppermute | solution.py:14
  418.3 4.4 copy-start.4
  419.2 2.2 copy-start.9
  421.4 1.3 copy-start.17
  422.7 2.2 copy-start.8
  424.9 4.6 copy-start.18
  429.5 4.0 slice-start.2
  433.7 12.3 %copy-start.25 = (bf16[256,768]{0,1:T(8,128)(2,1)}, bf16[256,768]{0,1:T(8,128)(2,1)S(1)}, u32[]{:S(2)}) copy-start(bf16[256,768]{0,1:T(8,128)(2,1)S(1)} %copy.62) | copy-start | bytes 1179652
  437.7 4.0 slice-start.3
  441.9 4.1 copy-start.30
  452.7 8.7 %copy-start.28 = (pred[1184]{0:T(1024)(128)(4,1)S(1)}, pred[1184]{0:T(1024)(128)(4,1)}, u32[]{:S(2)}) copy-start(pred[1184]{0:T(1024)(128)(4,1)} %copy-done.27) | copy-start | bytes 3556
  477.7 2.1 copy-start.5
  477.7 2.1 copy-start.24
  480.6 0.9 copy-start.10
  481.5 4.1 copy-start.26
  481.5 4.2 copy-start.14
  481.5 4.2 copy-start.15
  481.5 4.3 copy-start.16
  482.4 6.0 %collective-permute-start.1 = (bf16[2,256,768]{2,1,0:T(8,128)(2,1)}, bf16[2,256,768]{2,1,0:T(8,128)(2,1)}, u32[]{:S(2)}, u32[]{:S(2)}) collective-permute-start(bf16[2,256,768]{2,1,0:T(8,128)(2,1)} %fusion.94), channel_id=1, source_target_pairs={{128,0},{129,1},{130,2},{131,3},{132,4},{133,5},{134,6},{135,7},{1... | collective-permute-start | bytes 2359304 | tf_op jit(solution)/shard_map/ppermute | solution.py:14
  485.7 2.7 copy-start.3
  485.7 2.7 copy-start.11
Sparse Core Ops, SparseCore 0:
  12.3 144.0 all-gather.10
  160.8 111.1 all-gather.12
  273.7 42.6 all-gather.6
  318.1 42.2 all-gather.8
where the time goes:
time: 502 us; the launch traced here: 497 us
  waiting for transfers between devices  288 us (57%)
  matrix products  93.5 us (19%)
  local copies, waits for them, and re-layouts  76.1 us (15%)
  other arithmetic  19.8 us (4%)
  between operations  14.6 us (3%)
    all_gather x1, waiting for transfers between devices, body(): lax.all_gather(w_qkv[0], ('patch', 'req'), axis=0, tiled=True)  141 us
    all_gather x1, waiting for transfers between devices, body(): lax.all_gather(w_out[0], ('patch', 'req'), axis=0, tiled=True)  91.4 us
    all_gather x2, waiting for transfers between devices, process(): image_rows = lax.all_gather(patched, 'patch', axis=0, tiled=True)  52.2 us
    dot_general x4, matrix products, attend(): jnp.einsum('hqk,khd->qhd', soft_weights, value_heads, preferred_element_t...  36.9 us
    unnamed x74, local copies, waits for them, and re-layouts  27.8 us
    sub x4, matrix products, attend(): exp_scores = jnp.exp(scores - row_max)  27.6 us
    slice x4, local copies, waits for them, and re-layouts, process(): context[:, head_width:]  16.2 us
    slice x4, local copies, waits for them, and re-layouts, process(): context[:, :head_width]  15.8 us
  transfers between devices with their start and end apart: 6, of which 5 were waited for; matrix products, arithmetic and copies ran while one was open for 13% of the time, Pallas kernels for 0%

commit v1 on v0

--- a/solution.py
+++ b/solution.py
@@ -79,7 +79,9 @@
             held_norm, full_qkv[:, head_width:], preferred_element_type=jnp.float32
         ).astype(jnp.bfloat16)
         patched = stale_block.at[redo_index].set(redone)
-        image_rows = lax.all_gather(patched, "patch", axis=0, tiled=True)
+        image_rows = jnp.concatenate(
+            lax.all_to_all(jnp.stack([patched] * lax.axis_size("patch")), "patch", 0, 0), axis=0
+        )
         normed = modulate(layer_input, mod_rows[0], mod_rows[1])
         projected = jnp.dot(normed, full_qkv, preferred_element_type=jnp.float32).astype(
             jnp.bfloat16

time: 502 us -> 456 us (0.908)
  waiting for transfers between devices: 288 us -> 226 us
  starting transfers between devices: 4.55 us -> 13.6 us
    all_gather x2 -> x0, waiting for transfers between devices: 52.2 us -> none  [process(): image_rows = lax.all_gather(patched, 'patch', axis=0, tiled=True)]
    all_gather x1, waiting for transfers between devices: 91.4 us -> 56.6 us  [body(): lax.all_gather(w_out[0], ('patch', 'req'), axis=0, tiled=True)]
    all_to_all x0 -> x2, waiting for transfers between devices: none -> 25.7 us  [process(): lax.all_to_all(jnp.stack([patched] * lax.axis_size('patch')), 'patch', 0, 0)]
    all_to_all x0 -> x2, starting transfers between devices: none -> 9.14 us  [process(): lax.all_to_all(jnp.stack([patched] * lax.axis_size('patch')), 'patch', 0, 0)]
    another operation x0 -> x2, local copies, waits for them, and re-layouts: none -> 5.52 us  [process(): jnp.stack([patched] * lax.axis_size('patch'))]
  transfers between devices with their start and end apart: 6 -> 6, of which waited for: 5 -> 4; matrix products, arithmetic and copies ran while one was open for 13% -> 16% of each run, Pallas kernels for 0% -> 0%
where the time goes in v1:
time: 456 us; the launch traced here: 450 us
  waiting for transfers between devices  226 us (50%)
  matrix products  93.1 us (20%)
  local copies, waits for them, and re-layouts  79.4 us (17%)
  other arithmetic  23.2 us (5%)
  between operations  14.8 us (3%)
  starting transfers between devices  13.6 us (3%)
    all_gather x1, waiting for transfers between devices, body(): lax.all_gather(w_qkv[0], ('patch', 'req'), axis=0, tiled=True)  139 us
    all_gather x1, waiting for transfers between devices, body(): lax.all_gather(w_out[0], ('patch', 'req'), axis=0, tiled=True)  56.6 us
    dot_general x4, matrix products, attend(): jnp.einsum('hqk,khd->qhd', soft_weights, value_heads, preferred_element_t...  36.9 us
    sub x4, matrix products, attend(): exp_scores = jnp.exp(scores - row_max)  27.6 us
    unnamed x74, local copies, waits for them, and re-layouts  26.2 us
    all_to_all x2, waiting for transfers between devices, process(): lax.all_to_all(jnp.stack([patched] * lax.axis_size('patch')), 'patch', 0, 0)  25.7 us
    slice x4, local copies, waits for them, and re-layouts, process(): context[:, head_width:]  16.2 us
    slice x4, local copies, waits for them, and re-layouts, process(): context[:, :head_width]  15.8 us
  transfers between devices with their start and end apart: 6, of which 4 were waited for; matrix products, arithmetic and copies ran while one was open for 16% of the time, Pallas kernels for 0%

profile of v1, /device:TPU:1, one launch (start us, length us, event | category | flops | bytes accessed | tf_op | source)
XLA Modules:
  0.0 450.0 jit_solution(12473100011457481354)
XLA Ops:
  7.2 1.6 copy.50
  8.9 1.4 copy.54
  15.5 2.4 slice_bitcast_fusion
  17.9 138.6 %all-gather.5.cloned.1.call-done = bf16[1,1536,2304]{2,0,1:T(2,128)(2,1)} async-done(((bf16[1,12,2304]{2,0,1:T(2,128)(2,1)}), bf16[1,1536,2304]{2,0,1:T(2,128)(2,1)}) %all-gather.5.cloned.1.call-update) | async-done | bytes 7077904 | tf_op jit(solution)/shard_map/all_gather | solution.py:59
  156.4 9.0 %copy.67 = bf16[1,1536,2304]{2,1,0:T(8,128)(2,1)} copy(bf16[1,1536,2304]{2,0,1:T(2,128)(2,1)} %all-gather.5.cloned.1.call-done) | data formatting | bytes 14155776
  165.5 3.1 fusion.52
  169.8 1.9 stack.28
  171.7 4.0 all-to-all-start
  177.0 1.8 convert_reduce_fusion.3
  180.5 3.1 fusion.55
  183.6 2.9 scatter_fusion.1
  186.5 25.7 %all-to-all-done = bf16[4,256,1536]{2,1,0:T(8,128)(2,1)S(1)} async-done(((bf16[4,256,1536]{2,1,0:T(8,128)(2,1)}), bf16[4,256,1536]{2,1,0:T(8,128)(2,1)S(1)}, u32[]{:S(2)}, u32[]{:S(2)}) %all-to-all-start) | async-done | bytes 3145760 | tf_op jit(solution)/shard_map/all_to_all | solution.py:83
  212.1 3.6 stack.30
  215.8 5.2 %all-to-all-start.1 = ((bf16[4,256,1536]{2,1,0:T(8,128)(2,1)}), bf16[4,256,1536]{2,1,0:T(8,128)(2,1)}, u32[]{:S(2)}, u32[]{:S(2)}) async-start(bf16[4,256,1536]{2,1,0:T(8,128)(2,1)} %stack.30), calls=%async_computation.1 | async-start | bytes 6291456 | tf_op jit(solution)/shard_map/all_to_all | solution.py:83
  221.0 56.6 %all-gather.7.cloned.1.call-done = bf16[1,768,1536]{2,0,1:T(2,128)(2,1)} async-done(((bf16[1,6,1536]{2,0,1:T(2,128)(2,1)}), bf16[1,768,1536]{2,0,1:T(2,128)(2,1)}) %all-gather.7.cloned.1.call-update) | async-done | bytes 2359312 | tf_op jit(solution)/shard_map/all_gather | solution.py:60
  277.5 3.0 copy.65
  280.6 5.2 %convolution_convert_fusion.3 = bf16[256,2304]{1,0:T(8,128)(2,1)S(1)} fusion(bf16[1536,2304]{1,0:T(8,128)(2,1)} %bitcast.214, f32[1536]{0:T(1024)S(1)} %get-tuple-element.16, f32[1536]{0:T(1024)S(1)} %get-tuple-element.17, f32[256]{0:T(256)S(1)} %add_rsqrt_fusion.3, f32[256]{0:T(256)S(1)} %broadcast_multiply_fusion.3, bf16[2,256,1536]{2,1,0:T(8,128)(2,1)S(1)} %copy-done.3), kind=kOutput, calls=%fused_computation.46 | convolution fusion | flops 1814888448 | bytes 9062400 | tf_op jit(solution)/shard_map/dot_general | solution.py:86
  287.7 5.4 %convolution_convert_fusion.2 = bf16[256,2304]{1,0:T(8,128)(2,1)S(1)} fusion(bf16[1536,2304]{1,0:T(8,128)(2,1)} %bitcast.215, f32[1536]{0:T(1024)S(1)} %get-tuple-element.18, f32[1536]{0:T(1024)S(1)} %get-tuple-element.19, f32[256]{0:T(256)S(1)} %add_rsqrt_fusion.2, f32[256]{0:T(256)S(1)} %broadcast_multiply_fusion.2, bf16[2,256,1536]{2,1,0:T(8,128)(2,1)} %param.10), kind=kOutput, calls=%fused_computation.45 | convolution fusion | flops 1814888448 | bytes 9058304 | tf_op jit(solution)/shard_map/dot_general | solution.py:86
  295.1 4.0 copy.73
  300.2 2.0 pad_maximum_fusion.3
  302.2 3.9 copy.53
  306.1 3.9 copy.51
  310.1 3.8 copy.72
  315.2 3.9 pad_maximum_fusion.1
  319.2 3.9 copy.57
  323.1 4.1 copy.55
  327.2 6.9 %fusion.178 = f32[12,256]{1,0:T(8,128)S(1)} fusion(pred[1184]{0:T(1024)(128)(4,1)S(1)} %concatenate.35, bf16[256,12,64]{0,2,1:T(8,128)(2,1)} %bitcast.236, bf16[1184,12,64]{0,2,1:T(8,128)(2,1)} %bitcast.220), kind=kOutput, calls=%fused_computation.243 | convolution fusion | flops 480117920 | bytes 2225312 | tf_op jit(solution)/shard_map/sub | solution.py:38
  334.1 9.4 %fusion.93 = bf16[12,64,256]{2,1,0:T(8,128)(2,1)} fusion(bf16[1184,12,64]{0,2,1:T(8,128)(2,1)} %bitcast.222, f32[12,256]{1,0:T(8,128)S(1)} %fusion.178, pred[1184]{0:T(1024)(128)(4,1)S(1)} %concatenate.35, bf16[256,12,64]{0,2,1:T(8,128)(2,1)} %bitcast.237, bf16[1184,12,64]{0,2,1:T(8,128)(2,1)} %bitcast.221), kind=kOutput, calls=%fused_computation.131 | convolution fusion | flops 949522560 | bytes 4437152 | tf_op jit(solution)/shard_map/hqk,khd->qhd/dot_general | solution.py:40
  343.5 7.1 %fusion.177 = f32[12,256]{1,0:T(8,128)S(1)} fusion(pred[1184]{0:T(1024)(128)(4,1)S(1)} %concatenate.37, bf16[256,12,64]{0,2,1:T(8,128)(2,1)} %bitcast.238, bf16[1184,12,64]{0,2,1:T(8,128)(2,1)} %bitcast.227), kind=kOutput, calls=%fused_computation.242 | convolution fusion | flops 480117920 | bytes 2225312 | tf_op jit(solution)/shard_map/sub | solution.py:38
  350.6 9.5 %fusion.92 = bf16[12,64,256]{2,1,0:T(8,128)(2,1)} fusion(bf16[1184,12,64]{0,2,1:T(8,128)(2,1)} %bitcast.231, f32[12,256]{1,0:T(8,128)S(1)} %fusion.177, pred[1184]{0:T(1024)(128)(4,1)S(1)} %concatenate.37, bf16[256,12,64]{0,2,1:T(8,128)(2,1)} %bitcast.239, bf16[1184,12,64]{0,2,1:T(8,128)(2,1)} %bitcast.228), kind=kOutput, calls=%fused_computation.130 | convolution fusion | flops 949522560 | bytes 4437152 | tf_op jit(solution)/shard_map/hqk,khd->qhd/dot_general | solution.py:40
  360.1 2.2 fusion.39
  362.3 2.3 fusion.38
  366.1 5.0 %collective-permute-done = bf16[2,256,1536]{2,1,0:T(8,128)(2,1)S(1)} collective-permute-done((bf16[2,256,1536]{2,1,0:T(8,128)(2,1)S(1)}, bf16[2,256,1536]{2,1,0:T(8,128)(2,1)S(1)}, u32[]{:S(2)}, u32[]{:S(2)}) %collective-permute-start) | collective-permute-done | bytes 1572896 | tf_op jit(solution)/shard_map/ppermute | solution.py:14
  372.1 2.2 convolution_convert_fusion
  375.6 2.2 convolution_convert_fusion.1
  378.9 3.5 pad_maximum_fusion
  382.4 4.0 copy.63
  386.6 4.1 copy.61
  390.6 4.0 copy.60
  394.8 4.1 copy.58
  398.9 6.7 %fusion.180 = f32[12,256]{1,0:T(8,128)S(1)} fusion(pred[1184]{0:T(1024)(128)(4,1)S(1)} %copy-done.31, bf16[256,12,64]{0,2,1:T(8,128)(2,1)S(1)} %bitcast.242, bf16[1184,12,64]{0,2,1:T(8,128)(2,1)} %bitcast.225), kind=kOutput, calls=%fused_computation.245 | convolution fusion | flops 480117920 | bytes 2225312 | tf_op jit(solution)/shard_map/sub | solution.py:38
  405.6 8.7 %fusion.90 = bf16[12,64,256]{2,1,0:T(8,128)(2,1)S(1)} fusion(bf16[1184,12,64]{0,2,1:T(8,128)(2,1)} %bitcast.229, f32[12,256]{1,0:T(8,128)S(1)} %fusion.180, pred[1184]{0:T(1024)(128)(4,1)S(1)} %copy-done.31, bf16[256,12,64]{0,2,1:T(8,128)(2,1)} %bitcast.243, bf16[1184,12,64]{0,2,1:T(8,128)(2,1)} %bitcast.226), kind=kOutput, calls=%fused_computation.128 | convolution fusion | flops 949522560 | bytes 4437152 | tf_op jit(solution)/shard_map/hqk,khd->qhd/dot_general | solution.py:40
  414.3 7.0 %fusion.179 = f32[12,256]{1,0:T(8,128)S(1)} fusion(pred[1184]{0:T(1024)(128)(4,1)S(1)} %copy-done.29, bf16[256,12,64]{0,2,1:T(8,128)(2,1)S(1)} %bitcast.240, bf16[1184,12,64]{0,2,1:T(8,128)(2,1)} %bitcast.223), kind=kOutput, calls=%fused_computation.244 | convolution fusion | flops 480117920 | bytes 2225312 | tf_op jit(solution)/shard_map/sub | solution.py:38
  421.3 9.3 %fusion.91 = bf16[12,64,256]{2,1,0:T(8,128)(2,1)} fusion(bf16[1184,12,64]{0,2,1:T(8,128)(2,1)} %bitcast.230, f32[12,256]{1,0:T(8,128)S(1)} %fusion.179, pred[1184]{0:T(1024)(128)(4,1)S(1)} %copy-done.29, bf16[256,12,64]{0,2,1:T(8,128)(2,1)S(1)} %bitcast.241, bf16[1184,12,64]{0,2,1:T(8,128)(2,1)} %bitcast.224), kind=kOutput, calls=%fused_computation.129 | convolution fusion | flops 949522560 | bytes 4437152 | tf_op jit(solution)/shard_map/hqk,khd->qhd/dot_general | solution.py:40
  430.6 2.1 fusion.36
  435.3 3.1 collective-permute-start.1
  438.6 2.7 maximum_select_fusion
  441.3 1.6 multiply_add_fusion
  (120 shorter events, 23.7 us)
Async XLA Ops:
  7.2 149.3 %all-gather.5.cloned.1.call-start = ((), (), s32[]{:S(2)}) async-start(), calls=%async_computation.2 | async-start | bytes 14266368 | tf_op jit(solution)/shard_map/all_gather | solution.py:59
  8.8 268.7 %all-gather.7.cloned.1.call-start = ((), (), s32[]{:S(2)}) async-start(), calls=%async_computation.3 | async-start | bytes 4755456 | tf_op jit(solution)/shard_map/all_gather | solution.py:60
  17.9 147.6 %copy-start.24 = (bf16[1,2,24,1536]{3,2,1,0:T(8,128)(2,1)S(1)}, bf16[1,2,24,1536]{3,2,1,0:T(8,128)(2,1)}, u32[]{:S(2)}) copy-start(bf16[1,2,24,1536]{3,2,1,0:T(8,128)(2,1)} %param.17) | copy-start | bytes 442372
  171.7 40.4 %all-to-all-start = ((bf16[4,256,1536]{2,1,0:T(8,128)(2,1)}), bf16[4,256,1536]{2,1,0:T(8,128)(2,1)S(1)}, u32[]{:S(2)}, u32[]{:S(2)}) async-start(bf16[4,256,1536]{2,1,0:T(8,128)(2,1)} %stack.28), calls=%async_computation | async-start | bytes 6291456 | tf_op jit(solution)/shard_map/all_to_all | solution.py:83
  176.4 157.7 %copy-start.28 = (pred[1184]{0:T(1024)(128)(4,1)}, pred[1184]{0:T(1024)(128)(4,1)S(1)}, u32[]{:S(2)}) copy-start(pred[1184]{0:T(1024)(128)(4,1)S(1)} %concatenate.35) | copy-start | bytes 3556
  177.0 173.6 %copy-start.30 = (pred[1184]{0:T(1024)(128)(4,1)}, pred[1184]{0:T(1024)(128)(4,1)S(1)}, u32[]{:S(2)}) copy-start(pred[1184]{0:T(1024)(128)(4,1)S(1)} %concatenate.37) | copy-start | bytes 3556
  177.0 1.9 copy-start.2
  177.0 2.4 copy-start.23
  212.1 3.6 copy-start
  215.8 94.3 %all-to-all-start.1 = ((bf16[4,256,1536]{2,1,0:T(8,128)(2,1)}), bf16[4,256,1536]{2,1,0:T(8,128)(2,1)}, u32[]{:S(2)}, u32[]{:S(2)}) async-start(bf16[4,256,1536]{2,1,0:T(8,128)(2,1)} %stack.30), calls=%async_computation.1 | async-start | bytes 6291456 | tf_op jit(solution)/shard_map/all_to_all | solution.py:83
  277.5 3.0 copy-start.3
  285.7 1.0 copy-start.21
  293.1 1.0 copy-start.19
  295.1 4.0 copy-start.1
  295.1 4.0 copy-start.22
  299.1 1.1 copy-start.12
  310.1 3.9 copy-start.20
  313.9 1.3 copy-start.13
  360.1 2.2 copy-start.4
  360.1 11.9 %slice-start = ((s8[7077888]{0:T(1024)(128)(4,1)}), s8[4194304]{0:T(1024)(128)(4,1)S(1)}, s32[]{:S(2)}) async-start(s8[7077888]{0:T(1024)(128)(4,1)} %bitcast.216), calls=%async_computation.4 | async-start | bytes 8388608
  362.3 9.7 %slice-start.1 = ((s8[7077888]{0:T(1024)(128)(4,1)}), s8[2883584]{0:T(1024)(128)(4,1)S(1)}, s32[]{:S(2)}) async-start(s8[7077888]{0:T(1024)(128)(4,1)} %bitcast.216), calls=%async_computation.5 | async-start | bytes 5767168
  364.8 6.3 %collective-permute-start = (bf16[2,256,1536]{2,1,0:T(8,128)(2,1)S(1)}, bf16[2,256,1536]{2,1,0:T(8,128)(2,1)S(1)}, u32[]{:S(2)}, u32[]{:S(2)}) collective-permute-start(bf16[2,256,1536]{2,1,0:T(8,128)(2,1)S(1)} %pad_maximum_fusion.4), channel_id=1, source_target_pairs={{0,128},{1,129},{2,130},{3,131},{4,132},{5,133},{6,134},{7,135},{8... | collective-permute-start | bytes 4718600 | tf_op jit(solution)/shard_map/ppermute | solution.py:14
  371.2 4.4 copy-start.6
  372.1 2.2 copy-start.9
  374.3 1.3 copy-start.17
  375.6 2.2 copy-start.8
  377.8 4.6 %copy-start.18 = (bf16[256,2304]{1,0:T(8,128)(2,1)}, bf16[256,2304]{1,0:T(8,128)(2,1)S(1)}, u32[]{:S(2)}) copy-start(bf16[256,2304]{1,0:T(8,128)(2,1)S(1)} %convolution_convert_fusion.1) | copy-start | bytes 3538948
  382.4 4.0 slice-start.2
  386.6 12.3 %copy-start.26 = (bf16[256,768]{0,1:T(8,128)(2,1)}, bf16[256,768]{0,1:T(8,128)(2,1)S(1)}, u32[]{:S(2)}) copy-start(bf16[256,768]{0,1:T(8,128)(2,1)S(1)} %copy.62) | copy-start | bytes 1179652
  390.6 4.0 slice-start.3
  394.8 4.1 copy-start.31
  405.6 8.7 %copy-start.29 = (pred[1184]{0:T(1024)(128)(4,1)S(1)}, pred[1184]{0:T(1024)(128)(4,1)}, u32[]{:S(2)}) copy-start(pred[1184]{0:T(1024)(128)(4,1)} %copy-done.28) | copy-start | bytes 3556
  430.6 2.1 copy-start.7
  430.6 2.1 copy-start.25
  433.5 0.9 copy-start.10
  434.4 4.0 copy-start.27
  434.4 4.2 copy-start.14
  434.4 4.2 copy-start.15
  434.4 4.2 copy-start.16
  435.3 6.0 %collective-permute-start.1 = (bf16[2,256,768]{2,1,0:T(8,128)(2,1)}, bf16[2,256,768]{2,1,0:T(8,128)(2,1)}, u32[]{:S(2)}, u32[]{:S(2)}) collective-permute-start(bf16[2,256,768]{2,1,0:T(8,128)(2,1)} %fusion.94), channel_id=1, source_target_pairs={{128,0},{129,1},{130,2},{131,3},{132,4},{133,5},{134,6},{135,7},{1... | collective-permute-start | bytes 2359304 | tf_op jit(solution)/shard_map/ppermute | solution.py:14
  438.6 2.7 copy-start.5
  438.6 2.7 copy-start.11
Sparse Core Ops, SparseCore 0:
  12.3 144.0 all-gather.4
  160.2 117.2 all-gather.6
